TPU v7x, 512 devices: a whole 4x8x8 slice. The times are simulated.
512 devices in a mesh: dp: 16 (over x_lo, y), space: 32 (over x_hi, z, core).
Axes of the slice: x: 4 (x_hi: 2, x_lo: 2; x = x_hi * 2 + x_lo), y: 8, z: 8, core: 2. Of those that a mesh axis runs over, the one named last changes fastest.
Arguments:
- inputs: bfloat16 [16, 10, 64, 32, 128], P('dp', None, 'space'), may hold values from -8 to 8
- land_mask: int32 [16, 10, 64, 32], P('dp', None, 'space'), may hold values 0 or 1
- weight_one: float32 [128, 27, 128], P('dp'), may hold values from -0.109375 to 0.109375
- weight_two: float32 [128, 27, 128], P('dp'), may hold values from -0.109375 to 0.109375
- cotangent: bfloat16 [16, 10, 64, 32, 128], P('dp', None, 'space'), may hold values from -6 to 6
Outputs:
- prediction: bfloat16 [16, 10, 64, 32, 128], P('dp', None, 'space')
- input_grad: bfloat16 [16, 10, 64, 32, 128], P('dp', None, 'space')
- grad_one: float32 [128, 27, 128], P('dp')
- grad_two: float32 [128, 27, 128], P('dp')
All inputs are finite; a program needn't handle non-finite values. No bound on the sum of `land_mask` on one device may be relied on, other than what follows from the above.
Results may differ from a plain program's by a relative error of at most 0.0067.
Values may be sent and summed in bfloat16 or wider, within the bound.
No kernel may reach another device: no remote copies, remote signals or barrier semaphores. Data moves between devices by JAX's collectives and lax.ppermute only.
A program may use at most 64 MiB of HBM per device.

v0:
```python
import jax
import jax.numpy as jnp
from jax import lax
from jax.sharding import PartitionSpec as P


def with_halo(cells, sides, width):
    for axis, dim in sides:
        count = lax.axis_size(axis)
        ends = count - 1
        head = lax.slice_in_dim(cells, 0, width, axis=dim)
        tail = lax.slice_in_dim(cells, cells.shape[dim] - width, cells.shape[dim], axis=dim)
        cells = jnp.concatenate(
            [
                lax.ppermute(tail, axis, [(i, (i + 1) % count) for i in range(ends)]),
                cells,
                lax.ppermute(head, axis, [((i + 1) % count, i) for i in range(ends)]),
            ],
            axis=dim,
        )
    return cells


def widen(field):
    rimmed = with_halo(field, (("space", 2),), 1)
    return jnp.pad(rimmed, ((0, 0), (1, 1), (0, 0), (1, 1), (0, 0)))


def group_window(padded, depth_off, mirrored, shape):
    depth, rows, columns = shape
    pieces = []
    for row_off in range(3):
        for col_off in range(3):
            row_at = 2 - row_off if mirrored else row_off
            col_at = 2 - col_off if mirrored else col_off
            piece = padded[
                :,
                depth_off : depth_off + depth,
                row_at : row_at + rows,
                col_at : col_at + columns,
                :,
            ]
            pieces.append(piece.reshape(-1, padded.shape[4]))
    return jnp.concatenate(pieces, axis=1)


def conv_full(padded, kernel, shape):
    channel = kernel.shape[0]
    total = None
    for group in range(3):
        window = group_window(padded, group, False, shape)
        block = jnp.transpose(kernel[:, 9 * group : 9 * group + 9, :], (1, 0, 2)).reshape(
            9 * channel, kernel.shape[2]
        )
        term = jnp.dot(window, block, preferred_element_type=jnp.float32)
        total = term if total is None else total + term
    return total


def transpose_part(padded, kernel, shape):
    channel = kernel.shape[0]
    total = None
    for group in range(3):
        window = group_window(padded, 2 - group, True, shape)
        block = kernel[:, 9 * group : 9 * group + 9, :].reshape(channel, 9 * kernel.shape[2])
        term = lax.dot_general(
            window, block, (((1,), (1,)), ((), ())), preferred_element_type=jnp.float32
        )
        total = term if total is None else total + term
    return total


def local_grad(padded, back_flat, shape):
    channel = padded.shape[4]
    terms = []
    for group in range(3):
        window = group_window(padded, group, False, shape)
        block = lax.dot_general(
            window, back_flat, (((0,), (0,)), ((), ())), preferred_element_type=jnp.float32
        )
        terms.append(jnp.transpose(block.reshape(9, channel, back_flat.shape[1]), (1, 0, 2)))
    return jnp.concatenate(terms, axis=1)


def kernel_again(kernel):
    return lax.all_gather(kernel, "dp", axis=0, tiled=True)


def reduce_grad(grad_full):
    owned = lax.psum_scatter(grad_full, "dp", scatter_dimension=0, tiled=True)
    return lax.psum(owned, "space")


def on_device(inputs, land_mask, weight_one, weight_two, cotangent):
    samples, depth, rows, columns, channel = inputs.shape
    shape = (depth, rows, columns)
    kernel_one = weight_one.astype(jnp.bfloat16)
    kernel_two = weight_two.astype(jnp.bfloat16)
    scale = land_mask.reshape(-1, 1).astype(jnp.float32)
    in_pad = widen(inputs)
    pre_one = conv_full(in_pad, kernel_again(kernel_one), shape)
    act_one = (scale * jax.nn.silu(pre_one)).astype(jnp.bfloat16).reshape(inputs.shape)
    act_pad = widen(act_one)
    pre_two = conv_full(act_pad, kernel_again(kernel_two), shape)
    prediction = (scale * pre_two).astype(jnp.bfloat16).reshape(inputs.shape)
    back_two = (cotangent.reshape(-1, channel).astype(jnp.float32) * scale).astype(jnp.bfloat16)
    back_pad = widen(back_two.reshape(inputs.shape))
    grad_two = reduce_grad(local_grad(act_pad, back_two, shape))
    pull_one = transpose_part(back_pad, kernel_again(kernel_two), shape)
    sigma = jax.nn.sigmoid(pre_one)
    back_one = (pull_one * scale * sigma * (1.0 + pre_one * (1.0 - sigma))).astype(jnp.bfloat16)
    first_pad = widen(back_one.reshape(inputs.shape))
    grad_one = reduce_grad(local_grad(in_pad, back_one, shape))
    pulled = transpose_part(first_pad, kernel_again(kernel_one), shape)
    input_grad = pulled.astype(jnp.bfloat16).reshape(inputs.shape)
    return (prediction, input_grad, grad_one, grad_two)


def solution(mesh):
    in_specs = (
        P("dp", None, "space", None, None),
        P("dp", None, "space", None),
        P("dp", None, None),
        P("dp", None, None),
        P("dp", None, "space", None, None),
    )
    out_specs = (
        P("dp", None, "space", None, None),
        P("dp", None, "space", None, None),
        P("dp", None, None),
        P("dp", None, None),
    )
    return jax.shard_map(
        on_device, mesh=mesh, in_specs=in_specs, out_specs=out_specs, check_vma=False
    )
```

profile of v0, /device:TPU:1, one launch (start us, length us, event | category | flops | bytes accessed | tf_op | source)
XLA Modules:
  0.0 553.1 jit_solution(8356080933103198237)
XLA Ops:
  9.0 5.4 collective-permute-start.4
  14.4 4.7 collective-permute-start.5
  20.1 1.9 collective-permute-start
  22.0 2.4 collective-permute-start.1
  26.2 31.4 %all_gather.9 = bf16[128,27,128]{2,0,1:T(8,128)(2,1)S(1)} all-gather(bf16[8,27,128]{2,0,1:T(8,128)(2,1)S(1)} %convert_element_type.56), channel_id=1, replica_groups=mesh['dp'=16,'space'=32] {'dp'}, dimensions={0}, use_global_device_ids=true | all-gather | bytes 940032 | tf_op jit(solution)/shard_map/all_gather | solution.py:86
  57.7 28.5 %all_gather.8 = bf16[128,27,128]{2,0,1:T(8,128)(2,1)S(1)} all-gather(bf16[8,27,128]{2,0,1:T(8,128)(2,1)S(1)} %convert_element_type.54), channel_id=1, replica_groups=mesh['dp'=16,'space'=32] {'dp'}, dimensions={0}, use_global_device_ids=true | all-gather | bytes 940032 | tf_op jit(solution)/shard_map/all_gather | solution.py:86
  103.9 17.2 %collective-permute-start.2 = (bf16[1,10,1,32,128]{4,3,2,1,0:T(8,128)(2,1)S(1)}, bf16[1,10,1,32,128]{4,3,2,1,0:T(8,128)(2,1)S(1)}, u32[]{:S(2)}, u32[]{:S(2)}) collective-permute-start(bf16[1,10,1,32,128]{4,3,2,1,0:T(8,128)(2,1)S(1)} %get-tuple-element.118), channel_id=1, source_target_pairs={{0,1},{1,2},{2,3},{3,4},{4,5},{5,6},{6,7},{7,8},{8,9},{9,10},{10,1... | collective-permute-start | bytes 245768 | tf_op jit(solution)/shard_map/ppermute | solution.py:15
  121.1 1.9 collective-permute-start.3
  124.5 3.6 collective-permute-start.6
  128.1 2.1 collective-permute-start.7
  135.1 1.8 fusion.20
  141.9 1.7 copy.66
  143.6 1.7 copy.65
  145.3 1.7 copy.64
  147.0 1.7 copy.63
  157.1 1.6 constant_dynamic-update-slice_fusion.44
  160.4 1.6 constant_dynamic-update-slice_fusion.42
  162.0 1.6 constant_dynamic-update-slice_fusion.41
  167.2 3.7 copy.73
  170.8 1.7 constant_dynamic-update-slice_fusion.89
  172.5 1.6 constant_dynamic-update-slice_fusion.107
  174.2 1.6 pad_maximum_fusion.2
  182.0 1.8 constant_dynamic-update-slice_fusion.88
  183.8 1.7 constant_dynamic-update-slice_fusion.87
  185.5 1.7 constant_dynamic-update-slice_fusion.86
  187.1 1.7 constant_dynamic-update-slice_fusion.85
  188.8 1.7 constant_dynamic-update-slice_fusion.84
  190.5 1.6 constant_dynamic-update-slice_fusion.83
  196.6 2.0 convolution_add_fusion.5
  200.5 68.5 %reduce-scatter.5.cloned.1.call-done = f32[8,27,128]{2,0,1:T(8,128)} async-done(((f32[128,27,128]{2,0,1:T(8,128)}), f32[8,27,128]{2,0,1:T(8,128)}) %reduce-scatter.5.cloned.1.call-update) | async-done | bytes 110608 | tf_op jit(solution)/shard_map/reduce_scatter | solution.py:90
  270.2 273.3 %all-reduce.7.cloned.1.call-done = (f32[8,27,128]{2,0,1:T(8,128)}, f32[8,27,128]{2,0,1:T(8,128)}) async-done(((f32[8,27,128]{2,0,1:T(8,128)}, f32[8,27,128]{2,0,1:T(8,128)}), (f32[8,27,128]{2,0,1:T(8,128)}, f32[8,27,128]{2,0,1:T(8,128)})) %all-reduce.7.cloned.1.call-update) | async-done | bytes 221200 | tf_op jit(solution)/shard_map/psum | solution.py:91
  543.5 1.5 copy.172
  (309 shorter events, 61.3 us)
Async XLA Ops:
  7.2 193.3 %reduce-scatter.3.cloned.1.call-start = ((), (), s32[]{:S(2)}) async-start(), calls=%async_computation.2 | async-start | bytes 1880064 | tf_op jit(solution)/shard_map/reduce_scatter | solution.py:90
  9.0 83.1 %collective-permute-start.4 = (bf16[1,10,1,32,128]{4,3,2,1,0:T(8,128)(2,1)S(1)}, bf16[1,10,1,32,128]{4,3,2,1,0:T(8,128)(2,1)S(1)}, u32[]{:S(2)}, u32[]{:S(2)}) collective-permute-start(bf16[1,10,1,32,128]{4,3,2,1,0:T(8,128)(2,1)S(1)} %get-tuple-element.114), channel_id=1, source_target_pairs={{0,1},{1,2},{2,3},{3,4},{4,5},{5,6},{6,7},{7,8},{8,9},{9,10},{10,1... | collective-permute-start | bytes 245768 | tf_op jit(solution)/shard_map/ppermute | solution.py:15
  14.4 77.7 %collective-permute-start.5 = (bf16[1,10,1,32,128]{4,3,2,1,0:T(8,128)(2,1)S(1)}, bf16[1,10,1,32,128]{4,3,2,1,0:T(8,128)(2,1)S(1)}, u32[]{:S(2)}, u32[]{:S(2)}) collective-permute-start(bf16[1,10,1,32,128]{4,3,2,1,0:T(8,128)(2,1)S(1)} %get-tuple-element.115), channel_id=1, source_target_pairs={{1,0},{2,1},{3,2},{4,3},{5,4},{6,5},{7,6},{8,7},{9,8},{10,9},{11,1... | collective-permute-start | bytes 245768 | tf_op jit(solution)/shard_map/ppermute | solution.py:17
  20.1 71.1 %collective-permute-start = (bf16[1,10,1,32,128]{4,3,2,1,0:T(8,128)(2,1)S(1)}, bf16[1,10,1,32,128]{4,3,2,1,0:T(8,128)(2,1)S(1)}, u32[]{:S(2)}, u32[]{:S(2)}) collective-permute-start(bf16[1,10,1,32,128]{4,3,2,1,0:T(8,128)(2,1)S(1)} %get-tuple-element.122), channel_id=1, source_target_pairs={{0,1},{1,2},{2,3},{3,4},{4,5},{5,6},{6,7},{7,8},{8,9},{9,10},{10,1... | collective-permute-start | bytes 245768 | tf_op jit(solution)/shard_map/ppermute | solution.py:15
  22.0 69.1 %collective-permute-start.1 = (bf16[1,10,1,32,128]{4,3,2,1,0:T(8,128)(2,1)S(1)}, bf16[1,10,1,32,128]{4,3,2,1,0:T(8,128)(2,1)S(1)}, u32[]{:S(2)}, u32[]{:S(2)}) collective-permute-start(bf16[1,10,1,32,128]{4,3,2,1,0:T(8,128)(2,1)S(1)} %get-tuple-element.123), channel_id=1, source_target_pairs={{1,0},{2,1},{3,2},{4,3},{5,4},{6,5},{7,6},{8,7},{9,8},{10,9},{11,1... | collective-permute-start | bytes 245768 | tf_op jit(solution)/shard_map/ppermute | solution.py:17
  57.6 29.6 %copy-start.1 = (bf16[128,9,128]{2,0,1:T(8,128)(2,1)}, bf16[128,9,128]{2,0,1:T(8,128)(2,1)S(1)}, u32[]{:S(2)}) copy-start(bf16[128,9,128]{2,0,1:T(8,128)(2,1)S(1)} %get-tuple-element.6) | copy-start | bytes 884740
  57.7 29.6 %copy-start.3 = (bf16[128,9,128]{2,0,1:T(8,128)(2,1)}, bf16[128,9,128]{2,0,1:T(8,128)(2,1)S(1)}, u32[]{:S(2)}) copy-start(bf16[128,9,128]{2,0,1:T(8,128)(2,1)S(1)} %get-tuple-element.7) | copy-start | bytes 884740
  57.7 29.8 %copy-start.5 = (bf16[128,9,128]{2,0,1:T(8,128)(2,1)}, bf16[128,9,128]{2,0,1:T(8,128)(2,1)S(1)}, u32[]{:S(2)}) copy-start(bf16[128,9,128]{2,0,1:T(8,128)(2,1)S(1)} %get-tuple-element.8) | copy-start | bytes 884740
  103.9 26.3 %collective-permute-start.2 = (bf16[1,10,1,32,128]{4,3,2,1,0:T(8,128)(2,1)S(1)}, bf16[1,10,1,32,128]{4,3,2,1,0:T(8,128)(2,1)S(1)}, u32[]{:S(2)}, u32[]{:S(2)}) collective-permute-start(bf16[1,10,1,32,128]{4,3,2,1,0:T(8,128)(2,1)S(1)} %get-tuple-element.118), channel_id=1, source_target_pairs={{0,1},{1,2},{2,3},{3,4},{4,5},{5,6},{6,7},{7,8},{8,9},{9,10},{10,1... | collective-permute-start | bytes 245768 | tf_op jit(solution)/shard_map/ppermute | solution.py:15
  121.1 9.1 %collective-permute-start.3 = (bf16[1,10,1,32,128]{4,3,2,1,0:T(8,128)(2,1)S(1)}, bf16[1,10,1,32,128]{4,3,2,1,0:T(8,128)(2,1)S(1)}, u32[]{:S(2)}, u32[]{:S(2)}) collective-permute-start(bf16[1,10,1,32,128]{4,3,2,1,0:T(8,128)(2,1)S(1)} %get-tuple-element.119), channel_id=1, source_target_pairs={{1,0},{2,1},{3,2},{4,3},{5,4},{6,5},{7,6},{8,7},{9,8},{10,9},{11,1... | collective-permute-start | bytes 245768 | tf_op jit(solution)/shard_map/ppermute | solution.py:17
  124.4 144.5 %reduce-scatter.5.cloned.1.call-start = ((), (), s32[]{:S(2)}) async-start(), calls=%async_computation.3 | async-start | bytes 1880064 | tf_op jit(solution)/shard_map/reduce_scatter | solution.py:90
  124.5 8.9 %collective-permute-start.6 = (bf16[1,10,1,32,128]{4,3,2,1,0:T(8,128)(2,1)S(1)}, bf16[1,10,1,32,128]{4,3,2,1,0:T(8,128)(2,1)S(1)}, u32[]{:S(2)}, u32[]{:S(2)}) collective-permute-start(bf16[1,10,1,32,128]{4,3,2,1,0:T(8,128)(2,1)S(1)} %get-tuple-element.110), channel_id=1, source_target_pairs={{0,1},{1,2},{2,3},{3,4},{4,5},{5,6},{6,7},{7,8},{8,9},{9,10},{10,1... | collective-permute-start | bytes 245768 | tf_op jit(solution)/shard_map/ppermute | solution.py:15
  128.1 5.8 %collective-permute-start.7 = (bf16[1,10,1,32,128]{4,3,2,1,0:T(8,128)(2,1)S(1)}, bf16[1,10,1,32,128]{4,3,2,1,0:T(8,128)(2,1)S(1)}, u32[]{:S(2)}, u32[]{:S(2)}) collective-permute-start(bf16[1,10,1,32,128]{4,3,2,1,0:T(8,128)(2,1)S(1)} %get-tuple-element.111), channel_id=1, source_target_pairs={{1,0},{2,1},{3,2},{4,3},{5,4},{6,5},{7,6},{8,7},{9,8},{10,9},{11,1... | collective-permute-start | bytes 245768 | tf_op jit(solution)/shard_map/ppermute | solution.py:17
  156.1 8.2 %copy-start.37 = (bf16[1,10,2,32,128]{4,3,2,1,0:T(8,128)(2,1)S(1)}, bf16[1,10,2,32,128]{4,3,2,1,0:T(8,128)(2,1)}, u32[]{:S(2)}) copy-start(bf16[1,10,2,32,128]{4,3,2,1,0:T(8,128)(2,1)} %get-tuple-element.71) | copy-start | bytes 491524
  156.1 8.9 %copy-start.35 = (bf16[1,10,2,32,128]{4,3,2,1,0:T(8,128)(2,1)S(1)}, bf16[1,10,2,32,128]{4,3,2,1,0:T(8,128)(2,1)}, u32[]{:S(2)}) copy-start(bf16[1,10,2,32,128]{4,3,2,1,0:T(8,128)(2,1)} %get-tuple-element.70) | copy-start | bytes 491524
  158.7 7.8 %copy-start.33 = (bf16[1,10,2,32,128]{4,3,2,1,0:T(8,128)(2,1)S(1)}, bf16[1,10,2,32,128]{4,3,2,1,0:T(8,128)(2,1)}, u32[]{:S(2)}) copy-start(bf16[1,10,2,32,128]{4,3,2,1,0:T(8,128)(2,1)} %get-tuple-element.69) | copy-start | bytes 491524
  167.2 7.0 %copy-start.38 = (bf16[1,10,2,32,128]{4,3,2,1,0:T(8,128)(2,1)S(1)}, bf16[1,10,2,32,128]{4,3,2,1,0:T(8,128)(2,1)}, u32[]{:S(2)}) copy-start(bf16[1,10,2,32,128]{4,3,2,1,0:T(8,128)(2,1)} %get-tuple-element.26) | copy-start | bytes 491524
  170.8 5.1 copy-start.36
  170.8 5.1 copy-start.34
  170.8 5.3 copy-start.51
  181.9 10.2 %copy-start.32 = (bf16[1,10,2,32,128]{4,3,2,1,0:T(8,128)(2,1)S(1)}, bf16[1,10,2,32,128]{4,3,2,1,0:T(8,128)(2,1)}, u32[]{:S(2)}) copy-start(bf16[1,10,2,32,128]{4,3,2,1,0:T(8,128)(2,1)} %get-tuple-element.28) | copy-start | bytes 491524
  181.9 10.9 %copy-start.31 = (bf16[1,10,2,32,128]{4,3,2,1,0:T(8,128)(2,1)S(1)}, bf16[1,10,2,32,128]{4,3,2,1,0:T(8,128)(2,1)}, u32[]{:S(2)}) copy-start(bf16[1,10,2,32,128]{4,3,2,1,0:T(8,128)(2,1)} %get-tuple-element.27) | copy-start | bytes 491524
  181.9 11.6 %copy-start.30 = (bf16[1,10,2,32,128]{4,3,2,1,0:T(8,128)(2,1)S(1)}, bf16[1,10,2,32,128]{4,3,2,1,0:T(8,128)(2,1)}, u32[]{:S(2)}) copy-start(bf16[1,10,2,32,128]{4,3,2,1,0:T(8,128)(2,1)} %get-tuple-element.19) | copy-start | bytes 491524
  181.9 361.5 %all-reduce.7.cloned.1.call-start = ((), (), s32[]{:S(2)}) async-start(), calls=%async_computation.4 | async-start | bytes 442368 | tf_op jit(solution)/shard_map/psum | solution.py:91
  182.0 11.5 %copy-start.10 = (bf16[640,1152]{1,0:T(8,128)(2,1)S(1)}, bf16[640,1152]{1,0:T(8,128)(2,1)}, u32[]{:S(2)}) copy-start(bf16[640,1152]{1,0:T(8,128)(2,1)} %constant_dynamic-update-slice_fusion.107) | copy-start | bytes 4423684
  182.0 11.6 %copy-start.29 = (bf16[1,10,2,32,128]{4,3,2,1,0:T(8,128)(2,1)S(1)}, bf16[1,10,2,32,128]{4,3,2,1,0:T(8,128)(2,1)}, u32[]{:S(2)}) copy-start(bf16[1,10,2,32,128]{4,3,2,1,0:T(8,128)(2,1)} %get-tuple-element.18) | copy-start | bytes 491524
  183.8 9.9 %copy-start.28 = (bf16[1,10,2,32,128]{4,3,2,1,0:T(8,128)(2,1)S(1)}, bf16[1,10,2,32,128]{4,3,2,1,0:T(8,128)(2,1)}, u32[]{:S(2)}) copy-start(bf16[1,10,2,32,128]{4,3,2,1,0:T(8,128)(2,1)} %get-tuple-element.17) | copy-start | bytes 491524
  185.5 8.2 %copy-start.27 = (bf16[1,10,2,32,128]{4,3,2,1,0:T(8,128)(2,1)S(1)}, bf16[1,10,2,32,128]{4,3,2,1,0:T(8,128)(2,1)}, u32[]{:S(2)}) copy-start(bf16[1,10,2,32,128]{4,3,2,1,0:T(8,128)(2,1)} %get-tuple-element.16) | copy-start | bytes 491524
  187.1 6.7 %copy-start.26 = (bf16[1,10,2,32,128]{4,3,2,1,0:T(8,128)(2,1)S(1)}, bf16[1,10,2,32,128]{4,3,2,1,0:T(8,128)(2,1)}, u32[]{:S(2)}) copy-start(bf16[1,10,2,32,128]{4,3,2,1,0:T(8,128)(2,1)} %get-tuple-element.15) | copy-start | bytes 491524
  188.8 5.0 copy-start.25
  199.9 69.1 %copy-start.12 = (bf16[640,1152]{1,0:T(8,128)(2,1)S(1)}, bf16[640,1152]{1,0:T(8,128)(2,1)}, u32[]{:S(2)}) copy-start(bf16[640,1152]{1,0:T(8,128)(2,1)} %copy-done.11) | copy-start | bytes 4423684
  199.9 69.1 %copy-start.14 = (bf16[128,9,128]{0,2,1:T(8,128)(2,1)S(1)}, bf16[128,9,128]{0,2,1:T(8,128)(2,1)}, u32[]{:S(2)}) copy-start(bf16[128,9,128]{0,2,1:T(8,128)(2,1)} %copy.72) | copy-start | bytes 884740
  (45 other events, 66.7 us)
Sparse Core Ops, SparseCore 0:
  124.5 69.2 reduce-scatter.2
  196.9 72.0 reduce-scatter.4
  271.9 271.5 all-reduce.6
where the time goes:
time: 554 us; the launch traced here: 553 us
  waiting for transfers between devices  342 us (62%)
  local copies, waits for them, and re-layouts  73.7 us (13%)
  blocking collectives  59.9 us (11%)
  starting transfers between devices  39.4 us (7%)
  between operations  15.2 us (3%)
  matrix products  13 us (2%)
  other arithmetic  9.63 us (2%)
    psum x1, waiting for transfers between devices, reduce_grad(): return lax.psum(owned, 'space')  273 us
    reduce_scatter x2, waiting for transfers between devices, reduce_grad(): owned = lax.psum_scatter(grad_full, 'dp', scatter_dimension=0, tiled=True)  68.5 us
    all_gather x2, blocking collectives, kernel_again(): return lax.all_gather(kernel, 'dp', axis=0, tiled=True)  59.9 us
    unnamed x230, local copies, waits for them, and re-layouts  38.1 us
    ppermute x4, starting transfers between devices, with_halo(): lax.ppermute(tail, axis, [(i, (i + 1) % count) for i in range(ends)])  28.2 us
    reshape x18, local copies, waits for them, and re-layouts, group_window(): pieces.append(piece.reshape(-1, padded.shape[4]))  18.3 us
    ppermute x4, starting transfers between devices, with_halo(): lax.ppermute(head, axis, [((i + 1) % count, i) for i in range(ends)])  11.1 us
  transfers between devices with their start and end apart: 11, of which 3 were waited for; matrix products, arithmetic and copies ran while one was open for 14% of the time, Pallas kernels for 0%

commit v1 on v0

--- a/solution.py
+++ b/solution.py
@@ -1,7 +1,15 @@
+import functools
 import jax
 import jax.numpy as jnp
 from jax import lax
 from jax.sharding import PartitionSpec as P
+
+
+def _tell_ends(block_in, across):
+    return jnp.sum(lax.all_gather(block_in, across), axis=0)
+
+
+manage_the_body = functools.partial(_tell_ends, across="space")
 
 
 def with_halo(cells, sides, width):
@@ -88,7 +96,7 @@
 
 def reduce_grad(grad_full):
     owned = lax.psum_scatter(grad_full, "dp", scatter_dimension=0, tiled=True)
-    return lax.psum(owned, "space")
+    return manage_the_body(owned)
 
 
 def on_device(inputs, land_mask, weight_one, weight_two, cotangent):

time: 554 us -> 472 us (0.85)
  waiting for transfers between devices: 342 us -> 266 us
  local copies, waits for them, and re-layouts: 73.7 us -> 53.3 us
  starting transfers between devices: 39.4 us -> 50.8 us
    psum x1 -> x0, waiting for transfers between devices: 273 us -> none  [reduce_grad(): return lax.psum(owned, 'space')]
    all_gather x0 -> x2, waiting for transfers between devices: none -> 157 us  [_tell_ends(): return jnp.sum(lax.all_gather(block_in, across), axis=0)]
    reduce_scatter x2, waiting for transfers between devices: 68.5 us -> 107 us  [reduce_grad(): owned = lax.psum_scatter(grad_full, 'dp', scatter_dimension=0, tiled=True)]
    unnamed x230 -> x184, local copies, waits for them, and re-layouts: 38.1 us -> 15.6 us
    ppermute x4, starting transfers between devices: 28.2 us -> 39.6 us  [with_halo(): lax.ppermute(tail, axis, [(i, (i + 1) % count) for i in range(ends)])]
    reduce_sum x0 -> x2, other arithmetic: none -> 5.71 us  [_tell_ends(): return jnp.sum(lax.all_gather(block_in, across), axis=0)]
  transfers between devices with their start and end apart: 11 -> 12, of which waited for: 3 -> 5; matrix products, arithmetic and copies ran while one was open for 14% -> 12% of each run, Pallas kernels for 0% -> 0%
where the time goes in v1:
time: 472 us; the launch traced here: 471 us
  waiting for transfers between devices  266 us (56%)
  blocking collectives  59.9 us (13%)
  local copies, waits for them, and re-layouts  53.3 us (11%)
  starting transfers between devices  50.8 us (11%)
  between operations  15.2 us (3%)
  other arithmetic  13.7 us (3%)
  matrix products  11.6 us (2%)
    all_gather x2, waiting for transfers between devices, _tell_ends(): return jnp.sum(lax.all_gather(block_in, across), axis=0)  157 us
    reduce_scatter x2, waiting for transfers between devices, reduce_grad(): owned = lax.psum_scatter(grad_full, 'dp', scatter_dimension=0, tiled=True)  107 us
    all_gather x2, blocking collectives, kernel_again(): return lax.all_gather(kernel, 'dp', axis=0, tiled=True)  59.9 us
    ppermute x4, starting transfers between devices, with_halo(): lax.ppermute(tail, axis, [(i, (i + 1) % count) for i in range(ends)])  39.6 us
    reshape x18, local copies, waits for them, and re-layouts, group_window(): pieces.append(piece.reshape(-1, padded.shape[4]))  20.2 us
    unnamed x184, local copies, waits for them, and re-layouts  15.6 us
    ppermute x4, starting transfers between devices, with_halo(): lax.ppermute(head, axis, [((i + 1) % count, i) for i in range(ends)])  10.9 us
  transfers between devices with their start and end apart: 12, of which 5 were waited for; matrix products, arithmetic and copies ran while one was open for 12% of the time, Pallas kernels for 0%

profile of v1, /device:TPU:1, one launch (start us, length us, event | category | flops | bytes accessed | tf_op | source)
XLA Modules:
  0.0 470.7 jit_solution(3382744067351547471)
XLA Ops:
  9.0 5.4 %collective-permute-start.4 = (bf16[1,10,1,32,128]{4,3,2,1,0:T(8,128)(2,1)S(1)}, bf16[1,10,1,32,128]{4,3,2,1,0:T(8,128)(2,1)S(1)}, u32[]{:S(2)}, u32[]{:S(2)}) collective-permute-start(bf16[1,10,1,32,128]{4,3,2,1,0:T(8,128)(2,1)S(1)} %get-tuple-element.112), channel_id=1, source_target_pairs={{0,1},{1,2},{2,3},{3,4},{4,5},{5,6},{6,7},{7,8},{8,9},{9,10},{10,1... | collective-permute-start | bytes 245768 | tf_op jit(solution)/shard_map/ppermute | solution.py:23
  14.4 4.7 collective-permute-start.5
  20.1 1.9 collective-permute-start
  22.0 2.4 collective-permute-start.1
  26.2 31.4 %all_gather.21 = bf16[128,27,128]{2,0,1:T(8,128)(2,1)S(1)} all-gather(bf16[8,27,128]{2,0,1:T(8,128)(2,1)S(1)} %convert_element_type.56), channel_id=1, replica_groups=mesh['dp'=16,'space'=32] {'dp'}, dimensions={0}, use_global_device_ids=true | all-gather | bytes 940032 | tf_op jit(solution)/shard_map/all_gather | solution.py:94
  57.7 28.5 %all_gather.20 = bf16[128,27,128]{2,0,1:T(8,128)(2,1)S(1)} all-gather(bf16[8,27,128]{2,0,1:T(8,128)(2,1)S(1)} %convert_element_type.54), channel_id=1, replica_groups=mesh['dp'=16,'space'=32] {'dp'}, dimensions={0}, use_global_device_ids=true | all-gather | bytes 940032 | tf_op jit(solution)/shard_map/all_gather | solution.py:94
  105.0 17.2 %collective-permute-start.2 = (bf16[1,10,1,32,128]{4,3,2,1,0:T(8,128)(2,1)S(1)}, bf16[1,10,1,32,128]{4,3,2,1,0:T(8,128)(2,1)S(1)}, u32[]{:S(2)}, u32[]{:S(2)}) collective-permute-start(bf16[1,10,1,32,128]{4,3,2,1,0:T(8,128)(2,1)S(1)} %get-tuple-element.116), channel_id=1, source_target_pairs={{0,1},{1,2},{2,3},{3,4},{4,5},{5,6},{6,7},{7,8},{8,9},{9,10},{10,1... | collective-permute-start | bytes 245768 | tf_op jit(solution)/shard_map/ppermute | solution.py:23
  122.3 1.9 collective-permute-start.3
  124.2 1.4 pad_maximum_fusion
  125.8 2.2 collective-permute-done.3
  129.6 1.4 fusion.24
  131.0 1.8 copy.53
  132.8 1.7 copy.52
  134.5 1.7 copy.51
  136.2 1.7 copy.50
  137.9 1.7 copy.49
  139.7 1.7 copy.66
  152.6 2.1 copy.73
  161.7 1.3 pad_maximum_fusion.1
  163.2 31.8 %reduce-scatter.3.cloned.1.call-done = f32[8,27,128]{2,0,1:T(8,128)} async-done(((f32[128,27,128]{2,0,1:T(8,128)}), f32[8,27,128]{2,0,1:T(8,128)}) %reduce-scatter.3.cloned.1.call-update) | async-done | bytes 110608 | tf_op jit(solution)/shard_map/reduce_scatter | solution.py:98
  195.0 75.1 %reduce-scatter.5.cloned.1.call-done = f32[8,27,128]{2,0,1:T(8,128)} async-done(((f32[128,27,128]{2,0,1:T(8,128)}), f32[8,27,128]{2,0,1:T(8,128)}) %reduce-scatter.5.cloned.1.call-update) | async-done | bytes 110608 | tf_op jit(solution)/shard_map/reduce_scatter | solution.py:98
  270.2 15.0 %collective-permute-start.6 = (bf16[1,10,1,32,128]{4,3,2,1,0:T(8,128)(2,1)S(1)}, bf16[1,10,1,32,128]{4,3,2,1,0:T(8,128)(2,1)S(1)}, u32[]{:S(2)}, u32[]{:S(2)}) collective-permute-start(bf16[1,10,1,32,128]{4,3,2,1,0:T(8,128)(2,1)S(1)} %get-tuple-element.108), channel_id=1, source_target_pairs={{0,1},{1,2},{2,3},{3,4},{4,5},{5,6},{6,7},{7,8},{8,9},{9,10},{10,1... | collective-permute-start | bytes 245768 | tf_op jit(solution)/shard_map/ppermute | solution.py:23
  285.2 1.9 collective-permute-start.7
  287.1 1.9 copy.72
  289.0 1.9 copy.71
  290.8 1.9 copy.70
  298.1 1.2 fusion.6
  300.3 1.3 fusion.5
  301.6 70.1 %all-gather.5.cloned.1.call-done = f32[256,27,128]{2,0,1:T(8,128)} async-done(((f32[8,27,128]{2,0,1:T(8,128)}), f32[256,27,128]{2,0,1:T(8,128)}) %all-gather.5.cloned.1.call-update) | async-done | bytes 3538960 | tf_op jit(solution)/shard_map/all_gather | solution.py:9
  371.6 2.9 bitcast_reduce_fusion.1
  374.5 86.9 %all-gather.7.cloned.1.call-done = f32[256,27,128]{2,0,1:T(8,128)} async-done(((f32[8,27,128]{2,0,1:T(8,128)}), f32[256,27,128]{2,0,1:T(8,128)}) %all-gather.7.cloned.1.call-update) | async-done | bytes 3538960 | tf_op jit(solution)/shard_map/all_gather | solution.py:9
  461.3 2.9 bitcast_reduce_fusion
  (268 shorter events, 48.7 us)
Async XLA Ops:
  7.2 187.8 %reduce-scatter.3.cloned.1.call-start = ((), (), s32[]{:S(2)}) async-start(), calls=%async_computation.2 | async-start | bytes 1880064 | tf_op jit(solution)/shard_map/reduce_scatter | solution.py:98
  9.0 83.1 %collective-permute-start.4 = (bf16[1,10,1,32,128]{4,3,2,1,0:T(8,128)(2,1)S(1)}, bf16[1,10,1,32,128]{4,3,2,1,0:T(8,128)(2,1)S(1)}, u32[]{:S(2)}, u32[]{:S(2)}) collective-permute-start(bf16[1,10,1,32,128]{4,3,2,1,0:T(8,128)(2,1)S(1)} %get-tuple-element.112), channel_id=1, source_target_pairs={{0,1},{1,2},{2,3},{3,4},{4,5},{5,6},{6,7},{7,8},{8,9},{9,10},{10,1... | collective-permute-start | bytes 245768 | tf_op jit(solution)/shard_map/ppermute | solution.py:23
  14.4 77.7 %collective-permute-start.5 = (bf16[1,10,1,32,128]{4,3,2,1,0:T(8,128)(2,1)S(1)}, bf16[1,10,1,32,128]{4,3,2,1,0:T(8,128)(2,1)S(1)}, u32[]{:S(2)}, u32[]{:S(2)}) collective-permute-start(bf16[1,10,1,32,128]{4,3,2,1,0:T(8,128)(2,1)S(1)} %get-tuple-element.113), channel_id=1, source_target_pairs={{1,0},{2,1},{3,2},{4,3},{5,4},{6,5},{7,6},{8,7},{9,8},{10,9},{11,1... | collective-permute-start | bytes 245768 | tf_op jit(solution)/shard_map/ppermute | solution.py:25
  20.1 69.9 %collective-permute-start = (bf16[1,10,1,32,128]{4,3,2,1,0:T(8,128)(2,1)S(1)}, bf16[1,10,1,32,128]{4,3,2,1,0:T(8,128)(2,1)S(1)}, u32[]{:S(2)}, u32[]{:S(2)}) collective-permute-start(bf16[1,10,1,32,128]{4,3,2,1,0:T(8,128)(2,1)S(1)} %get-tuple-element.120), channel_id=1, source_target_pairs={{0,1},{1,2},{2,3},{3,4},{4,5},{5,6},{6,7},{7,8},{8,9},{9,10},{10,1... | collective-permute-start | bytes 245768 | tf_op jit(solution)/shard_map/ppermute | solution.py:23
  22.0 68.0 %collective-permute-start.1 = (bf16[1,10,1,32,128]{4,3,2,1,0:T(8,128)(2,1)S(1)}, bf16[1,10,1,32,128]{4,3,2,1,0:T(8,128)(2,1)S(1)}, u32[]{:S(2)}, u32[]{:S(2)}) collective-permute-start(bf16[1,10,1,32,128]{4,3,2,1,0:T(8,128)(2,1)S(1)} %get-tuple-element.121), channel_id=1, source_target_pairs={{1,0},{2,1},{3,2},{4,3},{5,4},{6,5},{7,6},{8,7},{9,8},{10,9},{11,1... | collective-permute-start | bytes 245768 | tf_op jit(solution)/shard_map/ppermute | solution.py:25
  57.7 30.5 %copy-start.3 = (bf16[128,9,128]{2,0,1:T(8,128)(2,1)}, bf16[128,9,128]{2,0,1:T(8,128)(2,1)S(1)}, u32[]{:S(2)}) copy-start(bf16[128,9,128]{2,0,1:T(8,128)(2,1)S(1)} %get-tuple-element.4) | copy-start | bytes 884740
  57.7 30.5 %copy-start.5 = (bf16[128,9,128]{2,0,1:T(8,128)(2,1)}, bf16[128,9,128]{2,0,1:T(8,128)(2,1)S(1)}, u32[]{:S(2)}) copy-start(bf16[128,9,128]{2,0,1:T(8,128)(2,1)S(1)} %get-tuple-element.5) | copy-start | bytes 884740
  57.7 31.4 %copy-start.8 = (bf16[128,9,128]{2,0,1:T(8,128)(2,1)}, bf16[128,9,128]{2,0,1:T(8,128)(2,1)S(1)}, u32[]{:S(2)}) copy-start(bf16[128,9,128]{2,0,1:T(8,128)(2,1)S(1)} %get-tuple-element.6) | copy-start | bytes 884740
  86.2 4.4 copy-start.11
  105.0 20.8 %collective-permute-start.2 = (bf16[1,10,1,32,128]{4,3,2,1,0:T(8,128)(2,1)S(1)}, bf16[1,10,1,32,128]{4,3,2,1,0:T(8,128)(2,1)S(1)}, u32[]{:S(2)}, u32[]{:S(2)}) collective-permute-start(bf16[1,10,1,32,128]{4,3,2,1,0:T(8,128)(2,1)S(1)} %get-tuple-element.116), channel_id=1, source_target_pairs={{0,1},{1,2},{2,3},{3,4},{4,5},{5,6},{6,7},{7,8},{8,9},{9,10},{10,1... | collective-permute-start | bytes 245768 | tf_op jit(solution)/shard_map/ppermute | solution.py:23
  122.3 5.8 %collective-permute-start.3 = (bf16[1,10,1,32,128]{4,3,2,1,0:T(8,128)(2,1)S(1)}, bf16[1,10,1,32,128]{4,3,2,1,0:T(8,128)(2,1)S(1)}, u32[]{:S(2)}, u32[]{:S(2)}) collective-permute-start(bf16[1,10,1,32,128]{4,3,2,1,0:T(8,128)(2,1)S(1)} %get-tuple-element.117), channel_id=1, source_target_pairs={{1,0},{2,1},{3,2},{4,3},{5,4},{6,5},{7,6},{8,7},{9,8},{10,9},{11,1... | collective-permute-start | bytes 245768 | tf_op jit(solution)/shard_map/ppermute | solution.py:25
  125.6 144.5 %reduce-scatter.5.cloned.1.call-start = ((), (), s32[]{:S(2)}) async-start(), calls=%async_computation.3 | async-start | bytes 1880064 | tf_op jit(solution)/shard_map/reduce_scatter | solution.py:98
  131.0 10.4 %copy-start.20 = (bf16[1,10,2,32,128]{4,3,2,1,0:T(8,128)(2,1)S(1)}, bf16[1,10,2,32,128]{4,3,2,1,0:T(8,128)(2,1)}, u32[]{:S(2)}) copy-start(bf16[1,10,2,32,128]{4,3,2,1,0:T(8,128)(2,1)} %get-tuple-element.59) | copy-start | bytes 491524
  131.0 11.2 %copy-start.19 = (bf16[1,10,2,32,128]{4,3,2,1,0:T(8,128)(2,1)S(1)}, bf16[1,10,2,32,128]{4,3,2,1,0:T(8,128)(2,1)}, u32[]{:S(2)}) copy-start(bf16[1,10,2,32,128]{4,3,2,1,0:T(8,128)(2,1)} %get-tuple-element.60) | copy-start | bytes 491524
  131.0 12.0 %copy-start.18 = (bf16[1,10,2,32,128]{4,3,2,1,0:T(8,128)(2,1)S(1)}, bf16[1,10,2,32,128]{4,3,2,1,0:T(8,128)(2,1)}, u32[]{:S(2)}) copy-start(bf16[1,10,2,32,128]{4,3,2,1,0:T(8,128)(2,1)} %get-tuple-element.61) | copy-start | bytes 491524
  152.6 2.1 copy-start.32
  152.6 5.2 %copy-start.28 = (bf16[640,128]{0,1:T(8,128)(2,1)S(1)}, bf16[640,128]{0,1:T(8,128)(2,1)}, u32[]{:S(2)}) copy-start(bf16[640,128]{0,1:T(8,128)(2,1)} %copy.52) | copy-start | bytes 491524
  154.7 3.1 copy-start.26
  154.7 3.2 copy-start.35
  154.7 3.2 copy-start.34
  154.7 3.3 copy-start.33
  154.7 3.3 copy-start.31
  154.7 3.3 copy-start.30
  155.8 2.3 copy-start.29
  158.1 1.7 copy-start
  163.1 208.5 %all-gather.5.cloned.1.call-start = ((), (), s32[]{:S(2)}) async-start(), calls=%async_computation.4 | async-start | bytes 3649536 | tf_op jit(solution)/shard_map/all_gather | solution.py:9
  195.0 266.4 %all-gather.7.cloned.1.call-start = ((), (), s32[]{:S(2)}) async-start(), calls=%async_computation.5 | async-start | bytes 3649536 | tf_op jit(solution)/shard_map/all_gather | solution.py:9
  270.2 22.5 %collective-permute-start.6 = (bf16[1,10,1,32,128]{4,3,2,1,0:T(8,128)(2,1)S(1)}, bf16[1,10,1,32,128]{4,3,2,1,0:T(8,128)(2,1)S(1)}, u32[]{:S(2)}, u32[]{:S(2)}) collective-permute-start(bf16[1,10,1,32,128]{4,3,2,1,0:T(8,128)(2,1)S(1)} %get-tuple-element.108), channel_id=1, source_target_pairs={{0,1},{1,2},{2,3},{3,4},{4,5},{5,6},{6,7},{7,8},{8,9},{9,10},{10,1... | collective-permute-start | bytes 245768 | tf_op jit(solution)/shard_map/ppermute | solution.py:23
  285.2 7.5 %collective-permute-start.7 = (bf16[1,10,1,32,128]{4,3,2,1,0:T(8,128)(2,1)S(1)}, bf16[1,10,1,32,128]{4,3,2,1,0:T(8,128)(2,1)S(1)}, u32[]{:S(2)}, u32[]{:S(2)}) collective-permute-start(bf16[1,10,1,32,128]{4,3,2,1,0:T(8,128)(2,1)S(1)} %get-tuple-element.109), channel_id=1, source_target_pairs={{1,0},{2,1},{3,2},{4,3},{5,4},{6,5},{7,6},{8,7},{9,8},{10,9},{11,1... | collective-permute-start | bytes 245768 | tf_op jit(solution)/shard_map/ppermute | solution.py:25
  294.5 1.4 copy-start.1
  294.5 1.4 copy-start.9
  294.8 1.7 copy-start.17
  (24 other events, 23.4 us)
Sparse Core Ops, SparseCore 0:
  125.7 69.1 reduce-scatter.2
  198.0 72.0 reduce-scatter.4
  273.3 98.2 all-gather.4
  374.6 86.6 all-gather.6
